TPU v7x, 512 devices: a whole 4x4x16 slice. The times are simulated.
512 devices in a mesh: space: 64 (over z_lo, x, core), ky: 8 (over z_hi, y).
Axes of the slice: x: 4, y: 4, z: 16 (z_hi: 2, z_lo: 8; z = z_hi * 8 + z_lo), core: 2. Of those that a mesh axis runs over, the one named last changes fastest.
Arguments:
- distribution: float32 [64, 128, 256, 128], P('space', 'ky'), may hold values from 0 to 2
- region: int32 [64, 256], P('space'), may hold values from 0 to 5, as said below
- region_doping: float32 [6], replicated, may hold values from -1 to 2
- region_relax: float32 [6], replicated, may hold values from 0.2 to 1
- equilibrium: float32 [128, 128], P('ky'), may hold values from 0.3 to 3
- kx_speed: float32 [128], replicated, may hold values from 0.1 to 1
- upwind_sign: int32 [128], replicated, may hold values from -1 to 1, as said below
Outputs:
- advanced: float32 [64, 128, 256, 128], P('space', 'ky')
Inputs may be any that keep to these rules, and one draw needn't show every extreme that they name: region[x, y] = 2 band(y) + m[x, y], with m[x, y] 0 or 1 and band(y) = 0, 1, 2 on three runs of columns, each run at least 32 columns long. `upwind_sign`: exactly 64 entries are 1 and the others -1.
All inputs are finite; a program needn't handle non-finite values.
Results may differ from a plain program's by a relative error of at most 0.0003.
Values sent between devices are 32-bit elements; how exact they have to be, the bound alone decides.
No kernel may reach another device: no remote copies, remote signals or barrier semaphores. Data moves between devices by JAX's collectives and lax.ppermute only.
A program may use at most 64 MiB of HBM per device.

v0:
```python
import math
import jax
import jax.numpy as jnp
from jax import lax
from jax.sharding import PartitionSpec as P

COUPLING = 0.04
POISSON = 0.1
STEP = 0.4
DRIFT_Y = 0.8


def with_halo(block, sides, width):
    for axis, dim in sides:
        count = lax.axis_size(axis)
        forward = [(i, i + 1) for i in range(count - 1)]
        backward = [(target, source) for source, target in forward]
        low = lax.ppermute(
            lax.slice_in_dim(block, block.shape[dim] - width, None, axis=dim), axis, forward
        )
        high = lax.ppermute(lax.slice_in_dim(block, 0, width, axis=dim), axis, backward)
        block = jnp.concatenate([low, block, high], axis=dim)
    return block


def sine_table(length):
    positions = jnp.arange(1, length + 1, dtype=jnp.int32)
    phase_index = positions[:, None] * positions[None, :] % (2 * length + 2)
    return jnp.sqrt(2.0 / (length + 1.0)) * jnp.sin(
        math.pi * phase_index.astype(jnp.float32) / (length + 1.0)
    )


def eigen_values(length):
    positions = jnp.arange(1, length + 1, dtype=jnp.int32).astype(jnp.float32)
    return 4.0 * jnp.sin(0.5 * math.pi * positions / (length + 1.0)) ** 2


def wigner_tables(modes):
    half_count = modes // 2
    shifts = jnp.arange(1, half_count + 1, dtype=jnp.int32)
    wave_index = jnp.arange(modes, dtype=jnp.int32)
    phase_index = shifts[:, None] * wave_index[None, :] % modes
    angles = 2.0 * math.pi / modes * phase_index.astype(jnp.float32)
    forward = jnp.concatenate([jnp.cos(angles), jnp.sin(angles)], axis=0)
    backward = jnp.concatenate([jnp.sin(angles).T, -jnp.cos(angles).T], axis=1)
    return (forward, backward)


def own_differences(potential, modes, first_col, local_cols):
    half_count = modes // 2
    padded = jnp.pad(potential, ((0, 0), (half_count, half_count)))
    window = lax.dynamic_slice_in_dim(padded, first_col, local_cols + 2 * half_count, 1)
    pieces = []
    for offset in range(1, half_count + 1):
        ahead_vals = window[:, half_count + offset : half_count + offset + local_cols]
        behind = window[:, half_count - offset : half_count - offset + local_cols]
        pieces.append(ahead_vals - behind)
    return COUPLING * jnp.stack(pieces, axis=1)


def lookup(region, values_table):
    classes = jnp.arange(values_table.shape[0], dtype=jnp.int32)
    return jnp.sum(jnp.where(region[..., None] == classes, values_table, 0.0), axis=-1)


def shards(distribution, region, region_doping, region_relax, equilibrium, kx_speed, upwind_sign):
    precise = lax.Precision.HIGHEST
    triple = lax.Precision.HIGH
    row_count, ky_local, col_count, kx_count = distribution.shape
    ky_count = ky_local * lax.axis_size("ky")
    grid_rows = row_count * lax.axis_size("space")
    row_start = lax.axis_index("space") * row_count
    partial_value = jnp.sum(distribution, axis=(1, 3)) / (ky_count * kx_count)
    density = lax.psum(partial_value, "ky")
    doping = lookup(region, region_doping)
    relax_rate = lookup(region, region_relax)
    charge = density - doping
    sine_rows = sine_table(grid_rows)
    sine_cols = sine_table(col_count)
    eigen_cols = eigen_values(col_count)
    every_row = lax.all_gather(charge, "space", axis=0, tiled=True)
    along_x = jnp.dot(sine_rows, every_row, precision=precise)
    spectral = jnp.dot(along_x, sine_cols, precision=precise)
    spectral = spectral / (eigen_values(grid_rows)[:, None] + eigen_cols[None, :])
    back_cols = jnp.dot(spectral, sine_cols, precision=precise)
    own_rows = lax.dynamic_slice_in_dim(sine_rows, row_start, row_count, 0)
    potential = POISSON * jnp.dot(own_rows, back_cols, precision=precise)
    spread = lax.all_to_all(distribution, "ky", split_axis=2, concat_axis=1, tiled=True)
    local_cols = spread.shape[2]
    forward, backward = wigner_tables(ky_count)
    weights = own_differences(potential, ky_count, lax.axis_index("ky") * local_cols, local_cols)
    flattened = spread.reshape(row_count, ky_count, local_cols * kx_count)
    coeffs = jnp.einsum("ab,rbm->ram", forward, flattened, precision=triple)
    coeffs = coeffs.reshape(row_count, ky_count, local_cols, kx_count)
    scaled = coeffs * jnp.concatenate([weights, weights], axis=1)[..., None]
    mixed = jnp.einsum(
        "ab,rbm->ram",
        backward,
        scaled.reshape(row_count, ky_count, local_cols * kx_count),
        precision=triple,
    )
    mixed = mixed.reshape(row_count, ky_count, local_cols, kx_count)
    wigner = lax.all_to_all(mixed, "ky", split_axis=1, concat_axis=2, tiled=True)
    positive_kx = upwind_sign > 0
    padded = with_halo(distribution, (("space", 0),), 1)
    from_left = padded[:-2]
    from_right = padded[2:]
    upstream_x = jnp.where(positive_kx[None, None, None, :], from_left, from_right)
    drift_x = -kx_speed[None, None, None, :] * (distribution - upstream_x)
    ky_global = lax.axis_index("ky") * ky_local + jnp.arange(ky_local, dtype=jnp.int32)
    upward = ky_global >= ky_count // 2
    vertical = DRIFT_Y * (ky_global.astype(jnp.float32) + 0.5 - 0.5 * ky_count) / (0.5 * ky_count)
    zero_col = jnp.zeros_like(distribution[:, :, :1])
    from_low = jnp.concatenate([zero_col, distribution[:, :, :-1]], axis=2)
    from_high = jnp.concatenate([distribution[:, :, 1:], zero_col], axis=2)
    upstream_y = jnp.where(upward[None, :, None, None], from_low, from_high)
    drift_y = -jnp.abs(vertical)[None, :, None, None] * (distribution - upstream_y)
    relaxation = relax_rate[:, None, :, None] * (
        density[:, None, :, None] * equilibrium[None, :, None, :] - distribution
    )
    return distribution + STEP * (drift_x + drift_y + wigner + relaxation)


def solution(mesh):
    return jax.shard_map(
        shards,
        mesh=mesh,
        in_specs=(
            P("space", "ky", None, None),
            P("space", None),
            P(),
            P(),
            P("ky", None),
            P(),
            P(),
        ),
        out_specs=P("space", "ky", None, None),
        check_vma=False,
    )
```

profile of v0, /device:TPU:32, one launch (start us, length us, event | category | flops | bytes accessed | tf_op | source)
XLA Modules:
  0.0 378.6 jit_solution(6376607305004779924)
XLA Ops:
  0.0 4.1 %copy.28 = f32[1,16,256,128]{3,1,0,2:T(8,128)} copy(f32[1,16,256,128]{3,2,1,0:T(8,128)} %param.7) | data formatting | bytes 4194304 | tf_op args[0]
  4.1 17.0 %all-to-all-start = ((f32[1,16,256,128]{3,1,0,2:T(8,128)}), f32[1,16,256,128]{3,1,0,2:T(8,128)}, u32[]{:S(2)}, u32[]{:S(2)}) async-start(f32[1,16,256,128]{3,1,0,2:T(8,128)} %copy.28), calls=%async_computation | async-start | bytes 4194304 | tf_op jit(solution)/shard_map/all_to_all | solution.py:89
  21.1 0.2 reduce_sum.29
  21.3 117.8 %psum.7 = f32[1,256]{1,0:T(1,128)S(1)} all-reduce(f32[1,256]{1,0:T(1,128)S(1)} %bitcast.205), channel_id=1, replica_groups=mesh['space'=64,'ky'=8] {'ky'}, use_global_device_ids=true, to_apply=%region_1.0 | all-reduce | flops 256 | bytes 2048 | tf_op jit(solution)/shard_map/psum | solution.py:75
  139.2 0.1 fusion.65
  139.3 105.4 %all-gather = f32[64,1,256]{2,1,0:T(1,128)S(1)} all-gather(f32[1,1,256]{2,1,0:T(1,128)S(1)} %subtract_bitcast_fusion), channel_id=1, replica_groups=mesh['space'=64,'ky'=8] {'space'}, dimensions={0}, use_global_device_ids=true | all-gather | bytes 66560 | tf_op jit(solution)/shard_map/all_gather | solution.py:82
  244.7 0.2 fusion.53
  245.0 0.4 fusion.39
  245.3 1.3 convolution_divide_fusion
  246.7 1.3 fusion.14
  248.0 0.1 fusion.67
  248.2 0.1 fusion.180
  248.3 0.1 copy.84
  248.4 0.1 fusion.174
  248.5 0.1 copy.81
  248.6 0.1 fusion.184
  248.7 0.1 copy.86
  248.8 0.1 fusion.194
  248.9 0.1 copy.91
  249.0 0.1 fusion.196
  249.1 0.1 copy.92
  249.2 0.1 fusion.172
  249.4 0.1 copy.80
  249.4 0.1 fusion.178
  249.6 0.1 copy.83
  249.7 0.1 fusion.186
  249.8 0.1 copy.87
  249.9 0.1 fusion.182
  250.0 0.1 copy.85
  250.1 0.1 fusion.170
  250.2 0.1 copy.79
  250.3 0.1 fusion.192
  250.4 0.1 copy.90
  250.5 0.1 fusion.176
  250.6 0.1 copy.82
  250.7 0.1 fusion.188
  250.8 0.1 copy.88
  250.9 0.1 fusion.168
  251.0 0.1 copy.78
  251.1 0.1 fusion.190
  251.3 0.1 fusion.70
  252.4 0.1 copy.34
  253.0 0.1 copy.57
  254.1 0.1 copy.59
  254.7 0.1 copy.64
  255.7 0.3 stack.259
  256.2 0.1 copy.94
  256.3 1.9 mul.263
  258.2 2.7 mul.264
  260.9 0.2 fusion.62
  261.1 0.3 fusion.54
  261.5 2.4 copy.29
  263.8 2.2 fusion.1
  266.0 3.2 fusion.35
  269.2 3.1 copy.95
  272.3 7.1 %all-to-all-start.1 = ((f32[1,128,32,128]{3,2,0,1:T(8,128)}), f32[1,128,32,128]{3,2,0,1:T(8,128)}, u32[]{:S(2)}, u32[]{:S(2)}) async-start(f32[1,128,32,128]{3,2,0,1:T(8,128)} %copy.95), calls=%async_computation.1 | async-start | bytes 4194304 | tf_op jit(solution)/shard_map/all_to_all | solution.py:104
  279.4 2.4 collective-permute-start.1
  281.8 1.9 collective-permute-start
  283.9 2.5 fusion.209
  286.3 46.5 %all-to-all-done.1 = f32[1,128,32,128]{3,2,0,1:T(8,128)} async-done(((f32[1,128,32,128]{3,2,0,1:T(8,128)}), f32[1,128,32,128]{3,2,0,1:T(8,128)}, u32[]{:S(2)}, u32[]{:S(2)}) %all-to-all-start.1) | async-done | bytes 2097184 | tf_op jit(solution)/shard_map/all_to_all | solution.py:104
  332.9 2.0 copy.96
  334.8 29.5 %collective-permute-done.1 = f32[1,16,256,128]{3,2,1,0:T(8,128)} collective-permute-done((f32[1,16,256,128]{3,2,1,0:T(8,128)S(1)}, f32[1,16,256,128]{3,2,1,0:T(8,128)}, u32[]{:S(2)}, u32[]{:S(2)}) %collective-permute-start.1) | collective-permute-done | bytes 2097184 | tf_op jit(solution)/shard_map/ppermute | solution.py:21
  364.3 8.7 %collective-permute-done = f32[1,16,256,128]{3,2,1,0:T(8,128)} collective-permute-done((f32[1,16,256,128]{3,2,1,0:T(8,128)S(1)}, f32[1,16,256,128]{3,2,1,0:T(8,128)}, u32[]{:S(2)}, u32[]{:S(2)}) %collective-permute-start) | collective-permute-done | bytes 2097184 | tf_op jit(solution)/shard_map/ppermute | solution.py:18
  373.1 5.5 %fusion.6 = f32[1,16,256,128]{3,2,1,0:T(8,128)} fusion(f32[1,16,256,128]{3,2,1,0:T(8,128)S(1)} %copy-done, f32[1,16,8,32,128]{4,3,2,1,0:T(8,128)S(1)} %copy.96, f32[1,16,255,128]{3,2,1,0:T(8,128)S(1)} %copy-done.3, f32[1,16,255,128]{3,2,1,0:T(8,128)S(1)} %copy-done.2, f32[1,16,256,128]{3,2,1,0:T(8,128)} %collective-permute-done, ...), kind=kLoop, calls=%fused_computation.8 | loop fusion | flops 7340032 | bytes 14674640 | tf_op jit(solution)/shard_map/add | solution.py:122
  (80 shorter events, 4.3 us)
Async XLA Ops:
  4.1 17.0 %copy-start = (f32[1,16,256,128]{3,2,1,0:T(8,128)S(1)}, f32[1,16,256,128]{3,2,1,0:T(8,128)}, u32[]{:S(2)}) copy-start(f32[1,16,256,128]{3,2,1,0:T(8,128)} %param.7) | copy-start | bytes 6291460
  4.1 257.3 %all-to-all-start = ((f32[1,16,256,128]{3,1,0,2:T(8,128)}), f32[1,16,256,128]{3,1,0,2:T(8,128)}, u32[]{:S(2)}, u32[]{:S(2)}) async-start(f32[1,16,256,128]{3,1,0,2:T(8,128)} %copy.28), calls=%async_computation | async-start | bytes 4194304 | tf_op jit(solution)/shard_map/all_to_all | solution.py:89
  21.1 118.1 %copy-start.5 = (s32[1,256]{1,0:T(1,128)S(1)}, s32[1,256]{1,0:T(1,128)}, u32[]{:S(2)}) copy-start(s32[1,256]{1,0:T(1,128)} %param.8) | copy-start | bytes 3076
  21.1 118.1 %copy-start.6 = (f32[6]{0:T(128)S(1)}, f32[6]{0:T(128)}, u32[]{:S(2)}) copy-start(f32[6]{0:T(128)} %param.10) | copy-start | bytes 76
  21.1 118.0 %copy-start.7 = (f32[6]{0:T(128)S(1)}, f32[6]{0:T(128)}, u32[]{:S(2)}) copy-start(f32[6]{0:T(128)} %param.9) | copy-start | bytes 76
  261.4 2.4 copy-start.1
  272.3 11.4 %copy-start.8 = (f32[128]{0:T(128)S(1)}, f32[128]{0:T(128)}, u32[]{:S(2)}) copy-start(f32[128]{0:T(128)} %param.12) | copy-start | bytes 1540
  272.3 11.5 %copy-start.9 = (s32[128]{0:T(128)S(1)}, s32[128]{0:T(128)}, u32[]{:S(2)}) copy-start(s32[128]{0:T(128)} %param.13) | copy-start | bytes 1540
  272.3 60.5 %all-to-all-start.1 = ((f32[1,128,32,128]{3,2,0,1:T(8,128)}), f32[1,128,32,128]{3,2,0,1:T(8,128)}, u32[]{:S(2)}, u32[]{:S(2)}) async-start(f32[1,128,32,128]{3,2,0,1:T(8,128)} %copy.95), calls=%async_computation.1 | async-start | bytes 4194304 | tf_op jit(solution)/shard_map/all_to_all | solution.py:104
  279.4 84.9 %collective-permute-start.1 = (f32[1,16,256,128]{3,2,1,0:T(8,128)S(1)}, f32[1,16,256,128]{3,2,1,0:T(8,128)}, u32[]{:S(2)}, u32[]{:S(2)}) collective-permute-start(f32[1,16,256,128]{3,2,1,0:T(8,128)S(1)} %copy-done), channel_id=1, source_target_pairs={{8,0},{16,8},{24,16},{32,24},{40,32},{48,40},{56,48},{64,56},{72,6... | collective-permute-start | bytes 6291464 | tf_op jit(solution)/shard_map/ppermute | solution.py:21
  281.8 91.2 %collective-permute-start = (f32[1,16,256,128]{3,2,1,0:T(8,128)S(1)}, f32[1,16,256,128]{3,2,1,0:T(8,128)}, u32[]{:S(2)}, u32[]{:S(2)}) collective-permute-start(f32[1,16,256,128]{3,2,1,0:T(8,128)S(1)} %copy-done), channel_id=1, source_target_pairs={{0,8},{8,16},{16,24},{24,32},{32,40},{40,48},{48,56},{56,64},{64,7... | collective-permute-start | bytes 6291464 | tf_op jit(solution)/shard_map/ppermute | solution.py:18
  283.8 89.2 %copy-start.4 = (f32[16,128]{1,0:T(8,128)S(1)}, f32[16,128]{1,0:T(8,128)}, u32[]{:S(2)}) copy-start(f32[16,128]{1,0:T(8,128)} %param.11) | copy-start | bytes 24580
  332.9 40.2 %copy-start.2 = (f32[1,16,255,128]{3,2,1,0:T(8,128)S(1)}, f32[1,16,255,128]{3,2,1,0:T(8,128)}, u32[]{:S(2)}) copy-start(f32[1,16,255,128]{3,2,1,0:T(8,128)} %get-tuple-element.7) | copy-start | bytes 6266884
  332.9 40.2 %copy-start.3 = (f32[1,16,255,128]{3,2,1,0:T(8,128)S(1)}, f32[1,16,255,128]{3,2,1,0:T(8,128)}, u32[]{:S(2)}) copy-start(f32[1,16,255,128]{3,2,1,0:T(8,128)} %get-tuple-element.8) | copy-start | bytes 6266884
where the time goes:
time: 379 us
  blocking collectives  223 us (59%)
  waiting for transfers between devices  84.8 us (22%)
  starting transfers between devices  28.4 us (7%)
  local copies, waits for them, and re-layouts  24.8 us (7%)
  other arithmetic  8.64 us (2%)
  matrix products  8.58 us (2%)
    psum x1, blocking collectives, shards(): density = lax.psum(partial_value, 'ky')  118 us
    all_gather x1, blocking collectives, shards(): every_row = lax.all_gather(charge, 'space', axis=0, tiled=True)  105 us
    all_to_all x1, waiting for transfers between devices, shards(): lax.all_to_all(mixed, 'ky', split_axis=1, concat_axis=2, tiled=True)  46.5 us
    ppermute x1, waiting for transfers between devices, with_halo(): lax.ppermute(lax.slice_in_dim(block, 0, width, axis=dim), axis, backward)  29.5 us
    all_to_all x1, starting transfers between devices, shards(): lax.all_to_all(distribution, 'ky', split_axis=2, concat_axis=1, tiled=True)  17 us
    ppermute x1, waiting for transfers between devices, with_halo(): lax.ppermute(lax.slice_in_dim(block, block.shape[dim] - width, None, axis...  8.73 us
  transfers between devices with their start and end apart: 4, of which 3 were waited for; matrix products, arithmetic and copies ran while one was open for 6% of the time, Pallas kernels for 0%

commit v1 on v0

--- a/solution.py
+++ b/solution.py
@@ -79,7 +79,9 @@
     sine_rows = sine_table(grid_rows)
     sine_cols = sine_table(col_count)
     eigen_cols = eigen_values(col_count)
-    every_row = lax.all_gather(charge, "space", axis=0, tiled=True)
+    every_row = jnp.concatenate(
+        lax.all_to_all(jnp.stack([charge] * lax.axis_size("space")), "space", 0, 0), axis=0
+    )
     along_x = jnp.dot(sine_rows, every_row, precision=precise)
     spectral = jnp.dot(along_x, sine_cols, precision=precise)
     spectral = spectral / (eigen_values(grid_rows)[:, None] + eigen_cols[None, :])

time: 379 us -> 321 us (0.85)
  the two profiles are of different devices: /device:TPU:32 before, /device:TPU:15 now
where the time goes in v1:
time: 321 us
  waiting for transfers between devices  176 us (55%)
  starting transfers between devices  67.1 us (21%)
  blocking collectives  34.2 us (11%)
  local copies, waits for them, and re-layouts  23.9 us (7%)
  other arithmetic  10.4 us (3%)
  matrix products  8.57 us (3%)
    ppermute x1, waiting for transfers between devices, with_halo(): lax.ppermute(lax.slice_in_dim(block, 0, width, axis=dim), axis, backward)  78.6 us
    all_to_all x1, waiting for transfers between devices, shards(): lax.all_to_all(distribution, 'ky', split_axis=2, concat_axis=1, tiled=True)  59.3 us
    psum x1, blocking collectives, shards(): density = lax.psum(partial_value, 'ky')  34.2 us
    all_to_all x1, waiting for transfers between devices, shards(): lax.all_to_all(mixed, 'ky', split_axis=1, concat_axis=2, tiled=True)  30.2 us
    ppermute x1, starting transfers between devices, with_halo(): lax.ppermute(lax.slice_in_dim(block, block.shape[dim] - width, None, axis...  20.6 us
    all_to_all x1, starting transfers between devices, shards(): lax.all_to_all(jnp.stack([charge] * lax.axis_size('space')), 'space', 0, 0)  15.9 us
    all_to_all x1, starting transfers between devices, shards(): lax.all_to_all(distribution, 'ky', split_axis=2, concat_axis=1, tiled=True)  13.9 us
    ppermute x1, starting transfers between devices, with_halo(): lax.ppermute(lax.slice_in_dim(block, 0, width, axis=dim), axis, backward)  11.9 us
  transfers between devices with their start and end apart: 5, of which 4 were waited for; matrix products, arithmetic and copies ran while one was open for 7% of the time, Pallas kernels for 0%

profile of v1, /device:TPU:15, one launch (start us, length us, event | category | flops | bytes accessed | tf_op | source)
XLA Modules:
  0.0 320.9 jit_solution(15993424353270809283)
XLA Ops:
  0.0 1.9 reduce_sum.29
  1.9 34.2 %psum.7 = f32[1,256]{1,0:T(1,128)S(1)} all-reduce(f32[1,256]{1,0:T(1,128)S(1)} %bitcast.205), channel_id=1, replica_groups=mesh['space'=64,'ky'=8] {'ky'}, use_global_device_ids=true, to_apply=%region_1.0 | all-reduce | flops 256 | bytes 2048 | tf_op jit(solution)/shard_map/psum | solution.py:75
  36.2 0.1 fusion.65
  36.3 0.7 stack.262
  37.0 15.9 %all-to-all-start.1 = ((f32[64,1,256]{2,1,0:T(1,128)}), f32[64,1,256]{2,1,0:T(1,128)S(1)}, u32[]{:S(2)}, u32[]{:S(2)}) async-start(f32[64,1,256]{2,1,0:T(1,128)} %stack.262), calls=%async_computation.1 | async-start | bytes 131072 | tf_op jit(solution)/shard_map/all_to_all | solution.py:83
  52.9 2.6 copy.28
  55.5 8.3 %all-to-all-done.1 = f32[64,1,256]{2,1,0:T(1,128)S(1)} async-done(((f32[64,1,256]{2,1,0:T(1,128)}), f32[64,1,256]{2,1,0:T(1,128)S(1)}, u32[]{:S(2)}, u32[]{:S(2)}) %all-to-all-start.1) | async-done | bytes 65568 | tf_op jit(solution)/shard_map/all_to_all | solution.py:83
  63.8 13.9 %all-to-all-start = ((f32[1,16,256,128]{3,1,0,2:T(8,128)}), f32[1,16,256,128]{3,1,0,2:T(8,128)}, u32[]{:S(2)}, u32[]{:S(2)}) async-start(f32[1,16,256,128]{3,1,0,2:T(8,128)} %copy.28), calls=%async_computation | async-start | bytes 4194304 | tf_op jit(solution)/shard_map/all_to_all | solution.py:91
  77.8 0.2 fusion.53
  78.1 0.2 fusion.62
  78.3 0.3 fusion.54
  78.6 0.4 fusion.39
  79.0 1.3 convolution_divide_fusion
  80.3 1.3 fusion.14
  81.6 0.1 fusion.67
  81.8 0.1 fusion.180
  81.9 0.1 copy.84
  82.0 0.1 fusion.174
  82.1 0.1 copy.81
  82.2 0.1 fusion.184
  82.3 0.1 copy.86
  82.4 0.1 fusion.194
  82.5 0.1 copy.91
  82.6 0.1 fusion.196
  82.8 0.1 copy.92
  82.8 0.1 fusion.172
  83.0 0.1 copy.80
  83.0 0.1 fusion.178
  83.2 0.1 copy.83
  83.3 0.1 fusion.186
  83.4 0.1 copy.87
  83.5 0.1 fusion.182
  83.6 0.1 copy.85
  83.7 0.1 fusion.170
  83.8 0.1 copy.79
  83.9 0.1 fusion.192
  84.0 0.1 copy.90
  84.1 0.1 fusion.176
  84.3 0.1 fusion.188
  84.5 0.1 fusion.168
  84.7 0.1 fusion.190
  84.9 0.1 fusion.70
  85.1 0.1 copy.66
  86.2 0.1 copy.62
  86.8 0.1 copy.50
  87.9 0.1 copy.36
  88.5 0.1 copy.41
  89.3 0.3 stack.327
  89.8 0.1 copy.94
  89.9 1.9 mul.263
  91.8 2.7 mul.264
  94.5 59.3 %all-to-all-done = f32[1,16,256,128]{3,1,0,2:T(8,128)} async-done(((f32[1,16,256,128]{3,1,0,2:T(8,128)}), f32[1,16,256,128]{3,1,0,2:T(8,128)}, u32[]{:S(2)}, u32[]{:S(2)}) %all-to-all-start) | async-done | bytes 2097184 | tf_op jit(solution)/shard_map/all_to_all | solution.py:91
  153.8 2.4 copy.29
  156.2 2.1 fusion.1
  158.4 3.2 fusion.35
  161.6 3.1 copy.95
  164.7 4.7 %all-to-all-start.2 = ((f32[1,128,32,128]{3,2,0,1:T(8,128)}), f32[1,128,32,128]{3,2,0,1:T(8,128)}, u32[]{:S(2)}, u32[]{:S(2)}) async-start(f32[1,128,32,128]{3,2,0,1:T(8,128)} %copy.95), calls=%async_computation.2 | async-start | bytes 4194304 | tf_op jit(solution)/shard_map/all_to_all | solution.py:106
  169.5 11.9 %collective-permute-start.1 = (f32[1,16,256,128]{3,2,1,0:T(8,128)S(1)}, f32[1,16,256,128]{3,2,1,0:T(8,128)}, u32[]{:S(2)}, u32[]{:S(2)}) collective-permute-start(f32[1,16,256,128]{3,2,1,0:T(8,128)S(1)} %copy-done), channel_id=1, source_target_pairs={{8,0},{16,8},{24,16},{32,24},{40,32},{48,40},{56,48},{64,56},{72,6... | collective-permute-start | bytes 6291464 | tf_op jit(solution)/shard_map/ppermute | solution.py:21
  181.3 20.6 %collective-permute-start = (f32[1,16,256,128]{3,2,1,0:T(8,128)S(1)}, f32[1,16,256,128]{3,2,1,0:T(8,128)}, u32[]{:S(2)}, u32[]{:S(2)}) collective-permute-start(f32[1,16,256,128]{3,2,1,0:T(8,128)S(1)} %copy-done), channel_id=1, source_target_pairs={{0,8},{8,16},{16,24},{24,32},{32,40},{40,48},{48,56},{56,64},{64,7... | collective-permute-start | bytes 6291464 | tf_op jit(solution)/shard_map/ppermute | solution.py:18
  202.1 2.5 fusion.209
  204.6 30.2 %all-to-all-done.2 = f32[1,128,32,128]{3,2,0,1:T(8,128)} async-done(((f32[1,128,32,128]{3,2,0,1:T(8,128)}), f32[1,128,32,128]{3,2,0,1:T(8,128)}, u32[]{:S(2)}, u32[]{:S(2)}) %all-to-all-start.2) | async-done | bytes 2097184 | tf_op jit(solution)/shard_map/all_to_all | solution.py:106
  234.8 2.0 copy.96
  236.7 78.6 %collective-permute-done.1 = f32[1,16,256,128]{3,2,1,0:T(8,128)} collective-permute-done((f32[1,16,256,128]{3,2,1,0:T(8,128)S(1)}, f32[1,16,256,128]{3,2,1,0:T(8,128)}, u32[]{:S(2)}, u32[]{:S(2)}) %collective-permute-start.1) | collective-permute-done | bytes 2097184 | tf_op jit(solution)/shard_map/ppermute | solution.py:21
  315.4 5.5 %fusion.6 = f32[1,16,256,128]{3,2,1,0:T(8,128)} fusion(f32[1,16,256,128]{3,2,1,0:T(8,128)S(1)} %copy-done, f32[1,16,8,32,128]{4,3,2,1,0:T(8,128)S(1)} %copy.96, f32[1,16,255,128]{3,2,1,0:T(8,128)S(1)} %copy-done.3, f32[1,16,255,128]{3,2,1,0:T(8,128)S(1)} %copy-done.2, f32[1,16,256,128]{3,2,1,0:T(8,128)} %collective-permute-done, ...), kind=kLoop, calls=%fused_computation.8 | loop fusion | flops 7340032 | bytes 14674640 | tf_op jit(solution)/shard_map/add | solution.py:124
  (82 shorter events, 4.4 us)
Async XLA Ops:
  0.0 52.9 %copy-start = (f32[1,16,256,128]{3,2,1,0:T(8,128)S(1)}, f32[1,16,256,128]{3,2,1,0:T(8,128)}, u32[]{:S(2)}) copy-start(f32[1,16,256,128]{3,2,1,0:T(8,128)} %param.7) | copy-start | bytes 6291460
  0.0 36.2 %copy-start.6 = (f32[6]{0:T(128)S(1)}, f32[6]{0:T(128)}, u32[]{:S(2)}) copy-start(f32[6]{0:T(128)} %param.10) | copy-start | bytes 76
  0.0 36.2 %copy-start.7 = (f32[6]{0:T(128)S(1)}, f32[6]{0:T(128)}, u32[]{:S(2)}) copy-start(f32[6]{0:T(128)} %param.9) | copy-start | bytes 76
  0.0 36.2 %copy-start.5 = (s32[1,256]{1,0:T(1,128)S(1)}, s32[1,256]{1,0:T(1,128)}, u32[]{:S(2)}) copy-start(s32[1,256]{1,0:T(1,128)} %param.8) | copy-start | bytes 3076
  37.0 26.9 %all-to-all-start.1 = ((f32[64,1,256]{2,1,0:T(1,128)}), f32[64,1,256]{2,1,0:T(1,128)S(1)}, u32[]{:S(2)}, u32[]{:S(2)}) async-start(f32[64,1,256]{2,1,0:T(1,128)} %stack.262), calls=%async_computation.1 | async-start | bytes 131072 | tf_op jit(solution)/shard_map/all_to_all | solution.py:83
  63.8 90.0 %all-to-all-start = ((f32[1,16,256,128]{3,1,0,2:T(8,128)}), f32[1,16,256,128]{3,1,0,2:T(8,128)}, u32[]{:S(2)}, u32[]{:S(2)}) async-start(f32[1,16,256,128]{3,1,0,2:T(8,128)} %copy.28), calls=%async_computation | async-start | bytes 4194304 | tf_op jit(solution)/shard_map/all_to_all | solution.py:91
  153.8 2.4 copy-start.1
  164.7 37.3 %copy-start.8 = (f32[128]{0:T(128)S(1)}, f32[128]{0:T(128)}, u32[]{:S(2)}) copy-start(f32[128]{0:T(128)} %param.12) | copy-start | bytes 1540
  164.7 37.3 %copy-start.9 = (s32[128]{0:T(128)S(1)}, s32[128]{0:T(128)}, u32[]{:S(2)}) copy-start(s32[128]{0:T(128)} %param.13) | copy-start | bytes 1540
  164.7 70.0 %all-to-all-start.2 = ((f32[1,128,32,128]{3,2,0,1:T(8,128)}), f32[1,128,32,128]{3,2,0,1:T(8,128)}, u32[]{:S(2)}, u32[]{:S(2)}) async-start(f32[1,128,32,128]{3,2,0,1:T(8,128)} %copy.95), calls=%async_computation.2 | async-start | bytes 4194304 | tf_op jit(solution)/shard_map/all_to_all | solution.py:106
  169.5 145.9 %collective-permute-start.1 = (f32[1,16,256,128]{3,2,1,0:T(8,128)S(1)}, f32[1,16,256,128]{3,2,1,0:T(8,128)}, u32[]{:S(2)}, u32[]{:S(2)}) collective-permute-start(f32[1,16,256,128]{3,2,1,0:T(8,128)S(1)} %copy-done), channel_id=1, source_target_pairs={{8,0},{16,8},{24,16},{32,24},{40,32},{48,40},{56,48},{64,56},{72,6... | collective-permute-start | bytes 6291464 | tf_op jit(solution)/shard_map/ppermute | solution.py:21
  181.3 134.0 %collective-permute-start = (f32[1,16,256,128]{3,2,1,0:T(8,128)S(1)}, f32[1,16,256,128]{3,2,1,0:T(8,128)}, u32[]{:S(2)}, u32[]{:S(2)}) collective-permute-start(f32[1,16,256,128]{3,2,1,0:T(8,128)S(1)} %copy-done), channel_id=1, source_target_pairs={{0,8},{8,16},{16,24},{24,32},{32,40},{40,48},{48,56},{56,64},{64,7... | collective-permute-start | bytes 6291464 | tf_op jit(solution)/shard_map/ppermute | solution.py:18
  202.1 113.3 %copy-start.4 = (f32[16,128]{1,0:T(8,128)S(1)}, f32[16,128]{1,0:T(8,128)}, u32[]{:S(2)}) copy-start(f32[16,128]{1,0:T(8,128)} %param.11) | copy-start | bytes 24580
  234.8 80.6 %copy-start.2 = (f32[1,16,255,128]{3,2,1,0:T(8,128)S(1)}, f32[1,16,255,128]{3,2,1,0:T(8,128)}, u32[]{:S(2)}) copy-start(f32[1,16,255,128]{3,2,1,0:T(8,128)} %get-tuple-element.7) | copy-start | bytes 6266884
  234.8 80.6 %copy-start.3 = (f32[1,16,255,128]{3,2,1,0:T(8,128)S(1)}, f32[1,16,255,128]{3,2,1,0:T(8,128)}, u32[]{:S(2)}) copy-start(f32[1,16,255,128]{3,2,1,0:T(8,128)} %get-tuple-element.8) | copy-start | bytes 6266884
